TPU v7x, 32 devices: a whole 2x2x4 slice. The times are simulated.
32 devices in a mesh: gx: 8 (over z, y), gy: 4 (over x, core).
Axes of the slice: x: 2, y: 2, z: 4, core: 2. Of those that a mesh axis runs over, the one named last changes fastest.
Arguments:
- records: bfloat16 [128, 8, 8192], P('gx', 'gy')
- kept_bins: int32 [1024], replicated, may hold values from 1 to 4095, as said below
- pair_offsets: int32 [128], replicated, may hold values from 1 to 128, as said below
Outputs:
- correlation: bfloat16 [128, 128, 512], P('gy', 'gx')
Inputs may be any that keep to these rules, and one draw needn't show every extreme that they name: `kept_bins`: 1024 different bin indices in increasing order, both 1 and 4095 among them. `pair_offsets`: each offset from 1 to 128 exactly once, in any order.
All inputs are finite; a program needn't handle non-finite values.
Results may differ from a plain program's by a relative error of at most 0.0075.
Values may be sent and summed in bfloat16 or wider, within the bound.
No kernel may reach another device: no remote copies, remote signals or barrier semaphores. Data moves between devices by JAX's collectives and lax.ppermute only.
A program may use at most 64 MiB of HBM per device.

v0:
```python
import math
import jax
import jax.numpy as jnp
from jax import lax
from jax.sharding import PartitionSpec as P

SAMPLES = 8192
LAGS = 512


def inverse_table(kept_bins):
    lag_index = jnp.arange(LAGS, dtype=jnp.int32) - LAGS // 2
    angles = jnp.mod(kept_bins[:, None] * lag_index[None, :], SAMPLES).astype(jnp.float32) * (
        2.0 * math.pi / SAMPLES
    )
    return jnp.stack([jnp.cos(angles), -jnp.sin(angles)], axis=0).astype(jnp.bfloat16)


def whiten(spectra):
    mean_power = jnp.mean(spectra * spectra, axis=-1, keepdims=True)
    return (spectra * lax.rsqrt(mean_power + 1e-06)).astype(jnp.bfloat16)


def add_cross(running, window_block, my_offsets, own_count):
    group_size = math.gcd(8, my_offsets.shape[0])
    own_part = window_block[:, :own_count].astype(jnp.float32)

    def one_offset(shift_by):
        theirs = lax.dynamic_slice_in_dim(window_block, shift_by, own_count, 1).astype(jnp.float32)
        real_part = jnp.sum(
            own_part[:, :, 0] * theirs[:, :, 0] + own_part[:, :, 1] * theirs[:, :, 1], axis=0
        )
        imag_part = jnp.sum(
            own_part[:, :, 1] * theirs[:, :, 0] - own_part[:, :, 0] * theirs[:, :, 1], axis=0
        )
        return jnp.stack([real_part, imag_part], axis=1)

    def one_group(group_index, carried):
        chosen = lax.dynamic_slice_in_dim(my_offsets, group_index * group_size, group_size)
        update = jax.vmap(one_offset)(chosen)
        current = lax.dynamic_slice_in_dim(carried, group_index * group_size, group_size, 0)
        return lax.dynamic_update_slice_in_dim(
            carried, current + update, group_index * group_size, 0
        )

    return lax.fori_loop(0, my_offsets.shape[0] // group_size, one_group, running)


def small_table(kept_bins, rows):
    fine_count = 1 << (rows.bit_length() - 1) // 2
    coarse_count = rows // fine_count

    def angles(step, count):
        index = step * jnp.arange(count, dtype=jnp.int32)
        return jnp.mod(index[:, None] * kept_bins[None, :], SAMPLES).astype(jnp.float32) * (
            2.0 * math.pi / SAMPLES
        )

    fine = angles(1, fine_count)[None, :, :]
    coarse = angles(fine_count, coarse_count)[:, None, :]
    cos_f, sin_f, cos_c, sin_c = (jnp.cos(fine), jnp.sin(fine), jnp.cos(coarse), jnp.sin(coarse))
    cos_t = cos_f * cos_c - sin_f * sin_c
    sin_t = sin_f * cos_c + cos_f * sin_c
    table = jnp.concatenate([cos_t, -sin_t], axis=-1)
    return table.reshape(rows, 2 * kept_bins.shape[0]).astype(jnp.bfloat16)


def forward_spectra(record_rows, kept_bins):
    row_count, samples = record_rows.shape
    bin_count = kept_bins.shape[0]
    block_len = math.gcd(samples, 1024)
    block_count = samples // block_len
    x = record_rows.reshape(row_count, block_count, block_len).astype(jnp.float32)
    br = jnp.mod(
        jnp.arange(block_count, dtype=jnp.int32)[:, None]
        * jnp.arange(block_count, dtype=jnp.int32)[None, :],
        block_count,
    ).astype(jnp.float32) * (2.0 * math.pi / block_count)
    twiddle = jnp.stack([jnp.cos(br), -jnp.sin(br)], axis=0)
    y = jnp.einsum("ubs,pbr->prus", x, twiddle, precision=lax.Precision.HIGHEST)
    y_hi = y.astype(jnp.bfloat16)
    y_lo = (y - y_hi.astype(jnp.float32)).astype(jnp.bfloat16)
    lhs = jnp.stack([y_hi, y_lo], axis=0).reshape(-1, block_len)
    prod = jnp.dot(lhs, small_table(kept_bins, block_len), preferred_element_type=jnp.float32)
    prod = prod.reshape(2, 2, block_count, row_count, 2, bin_count)
    prod = prod[0] + prod[1]
    pick = (
        jnp.mod(kept_bins, block_count)[None, None, :]
        == jnp.arange(block_count, dtype=jnp.int32)[:, None, None]
    ).astype(jnp.float32)
    real_part = jnp.sum(pick * (prod[0, :, :, 0] - prod[1, :, :, 1]), axis=0)
    imag_part = jnp.sum(pick * (prod[0, :, :, 1] + prod[1, :, :, 0]), axis=0)
    return jnp.concatenate([real_part, imag_part], axis=-1)


def local(records, kept_bins, pair_offsets):
    ch_dev, win_dev, samples = records.shape
    bin_count = kept_bins.shape[0]
    band_span = pair_offsets.shape[0]
    record_rows = jnp.transpose(records, (1, 0, 2)).reshape(win_dev * ch_dev, samples)
    spectra = forward_spectra(record_rows, kept_bins)
    white = whiten(spectra).reshape(win_dev, ch_dev, 2, bin_count)
    off_dev = band_span // lax.axis_size("gy")
    my_offsets = lax.dynamic_slice_in_dim(pair_offsets, lax.axis_index("gy") * off_dev, off_dev)
    inverse = inverse_table(kept_bins)
    norm_scale = 0.5 / math.sqrt(win_dev * lax.axis_size("gy") * bin_count)
    freq_white = lax.all_to_all(white, "gx", split_axis=3, concat_axis=1, tiled=True)
    all_channels = freq_white.shape[1]
    empty_sum = jnp.zeros((off_dev, all_channels, 2, freq_white.shape[3]), jnp.float32)
    window_block = lax.all_gather(freq_white, "gy", axis=0, tiled=True)
    widened = jnp.concatenate(
        [
            window_block,
            jnp.zeros(
                (window_block.shape[0], band_span, 2, window_block.shape[3]), window_block.dtype
            ),
        ],
        axis=1,
    )
    cross_sum = add_cross(empty_sum, widened, my_offsets, all_channels).astype(jnp.bfloat16)
    lagged = (
        jnp.einsum(
            "ocpk,pkl->ocl",
            lax.all_to_all(cross_sum, "gx", split_axis=1, concat_axis=3, tiled=True),
            inverse,
            preferred_element_type=jnp.float32,
        )
        * norm_scale
    )
    return lagged.astype(jnp.bfloat16)


def solution(mesh):
    return jax.shard_map(
        local,
        mesh=mesh,
        in_specs=(P("gx", "gy", None), P(), P()),
        out_specs=P("gy", "gx", None),
        check_vma=False,
    )
```

profile of v0, /device:TPU:0, one launch (start us, length us, event | category | flops | bytes accessed | tf_op | source)
XLA Modules:
  0.0 180.3 jit_solution(6627129745590901906)
XLA Ops:
  0.1 0.7 add_select_fusion.4
  0.8 1.7 fusion.32
  2.5 1.3 copy.39
  4.1 1.0 convert_bitcast_fusion
  5.4 1.2 copy.40
  6.5 1.5 subtract_convert_fusion
  8.0 4.5 %fusion.2 = f32[1024,2048]{1,0:T(8,128)S(1)} fusion(bf16[1024,1024]{1,0:T(8,128)(2,1)S(1)} %bitcast.101, bf16[1024,1024]{1,0:T(8,128)(2,1)S(1)} %bitcast.103, bf16[1024,1024]{1,0:T(8,128)(2,1)S(1)} %bitcast.102), kind=kOutput, calls=%fused_computation.14 | convolution fusion | flops 4303355904 | bytes 14680064 | tf_op jit(solution)/shard_map/dot_general | solution.py:84
  12.6 2.7 %slice_add_fusion = f32[512,2048]{1,0:T(8,128)} fusion(f32[1024,2048]{1,0:T(8,128)S(1)} %fusion.2), kind=kLoop, calls=%fused_computation.13 | loop fusion | flops 1048576 | bytes 12582912 | tf_op jit(solution)/shard_map/add | solution.py:86
  15.2 6.6 %add.157 = f32[2,8,32,2,1024]{4,3,2,1,0:T(2,128)} reshape(f32[512,2048]{1,0:T(8,128)} %slice_add_fusion) | data formatting | bytes 8388608 | tf_op jit(solution)/shard_map/add | solution.py:86
  21.8 6.9 %slice_add_fusion.1 = (f32[1,8,32,1,1024]{4,3,2,1,0:T(1,128)S(1)}, f32[1,8,32,1,1024]{4,3,2,1,0:T(1,128)S(1)}, f32[1,8,32,1,1024]{4,3,2,1,0:T(1,128)S(1)}) fusion(f32[2,8,32,2,1024]{4,3,2,1,0:T(2,128)} %add.157), kind=kLoop, calls=%fused_computation.41 | loop fusion | flops 262144 | bytes 7340032 | tf_op jit(solution)/shard_map/add | solution.py:92
  28.7 0.8 fusion.18
  30.1 0.8 copy.43
  30.9 1.7 reshape.414
  32.7 7.3 %all-to-all-start = ((bf16[8,2,4096]{2,1,0:T(2,128)(2,1)}), bf16[8,2,4096]{2,1,0:T(2,128)(2,1)S(1)}, u32[]{:S(2)}, u32[]{:S(2)}) async-start(bf16[8,2,4096]{2,1,0:T(2,128)(2,1)} %reshape.414), calls=%async_computation | async-start | bytes 262144 | tf_op jit(solution)/shard_map/all_to_all | solution.py:107
  40.0 7.3 %all-to-all-done = bf16[8,2,4096]{2,1,0:T(2,128)(2,1)S(1)} async-done(((bf16[8,2,4096]{2,1,0:T(2,128)(2,1)}), bf16[8,2,4096]{2,1,0:T(2,128)(2,1)S(1)}, u32[]{:S(2)}, u32[]{:S(2)}) %all-to-all-start) | async-done | bytes 131104 | tf_op jit(solution)/shard_map/all_to_all | solution.py:107
  47.3 0.7 reshape.415
  48.0 1.3 copy.53
  49.3 7.2 %all_gather.3 = bf16[8,128,2,128]{3,1,2,0:T(8,128)(2,1)S(1)} all-gather(bf16[2,128,2,128]{3,1,2,0:T(8,128)(2,1)S(1)} %bitcast.105), channel_id=1, replica_groups=mesh['gx'=8,'gy'=4] {'gy'}, dimensions={0}, use_global_device_ids=true | all-gather | bytes 655360 | tf_op jit(solution)/shard_map/all_gather | solution.py:110
  56.5 0.3 copy.64
  57.3 4.0 %broadcast_in_dim.8.clone = f32[32,128,2,128]{3,2,0,1:T(2,128)} broadcast(f32[]{:T(128)} %constant.108.clone.1), dimensions={} | broadcast | bytes 4194308 | tf_op jit(solution)/shard_map/broadcast_in_dim | solution.py:109
  61.3 51.1 %while.13 = (s32[]{:T(128)}, f32[32,128,2,128]{3,2,0,1:T(2,128)}, f32[8,128,2,128]{3,0,1,2:T(8,128)S(1)}, s32[32]{0:T(128)S(1)}, bf16[8,256,2,128]{3,0,2,1:T(8,1...) while((s32[]{:T(128)}, f32[32,128,2,128]{3,2,0,1:T(2,128)}, ...), condition=%wide.region_6.7_spmd, body=%wide.region_3.6_spmd.sunk | while | flops 10747950 | bytes 38797656 | solution.py:46
  61.4 3.1 %gather_fusion = bf16[8,8,128,2,128]{4,1,3,2,0:T(8,128)(2,1)} fusion(bf16[8,256,2,128]{3,0,2,1:T(8,128)(2,1)S(1)} %get-tuple-element.219, s32[8]{0:T(128)S(1)} %fusion.52), kind=kCustom, calls=%fused_computation.clone.1 | custom fusion | bytes 8388736 | tf_op jit(solution)/shard_map/while/body/eval_jaxpr/vmap()/gather | solution.py:29
  64.5 2.9 %convert_element_type.142 = f32[8,8,128,2,128]{4,1,3,2,0:T(8,128)S(1)} convert(bf16[8,8,128,2,128]{4,1,3,2,0:T(8,128)(2,1)} %gather_fusion) | non-fusion elementwise | flops 2097152 | bytes 12582912 | tf_op jit(solution)/shard_map/while/body/eval_jaxpr/vmap()/convert_element_type | solution.py:29
  67.5 3.1 %add_reduce_fusion.2 = (f32[8,128,128]{2,1,0:T(8,128)S(1)}, f32[8,128,128]{2,1,0:T(8,128)S(1)}) fusion(f32[8,8,128,2,128]{4,1,3,2,0:T(8,128)S(1)} %convert_element_type.142, f32[8,128,128]{2,0,1:T(8,128)S(1)} %get-tuple-element.193, f32[8,128,128]{2,0,1:T(8,128)S(1)} %get-tuple-element.194), kind=kLoop, calls=%fused_computation.4.clone.1 | loop fusion | flops 8126464 | bytes 10485760 | tf_op jit(solution)/shard_map/while/body/eval_jaxpr/vmap()/reduce_sum | solution.py:30
  70.6 1.3 constant_dynamic-slice_fusion.2
  71.9 2.2 %copy_dynamic-update-slice_fusion.2 = f32[32,128,2,128]{3,2,0,1:T(2,128)} fusion(f32[32,128,2,128]{3,2,0,1:T(2,128)} %get-tuple-element.207, s32[]{:T(128)S(6)} %select_n.137, f32[8,128,1,128]{3,2,1,0:T(1,128)S(1)} %bitcast.95, f32[8,128,1,128]{3,2,1,0:T(1,128)S(1)} %bitcast.94, f32[8,128,2,128]{3,2,0,1:T(2,128)S(1)} %constant_dynamic-slice_fusion.2), kind=kLoop, calls=%fused_computation.6.clone.1 | loop fusion | flops 524288 | bytes 3145732 | tf_op jit(solution)/shard_map/while/body/eval_jaxpr/dynamic_update_slice | solution.py:42
  74.2 3.1 %gather_fusion = bf16[8,8,128,2,128]{4,1,3,2,0:T(8,128)(2,1)} fusion(bf16[8,256,2,128]{3,0,2,1:T(8,128)(2,1)S(1)} %get-tuple-element.219, s32[8]{0:T(128)S(1)} %fusion.52), kind=kCustom, calls=%fused_computation.clone.1 | custom fusion | bytes 8388736 | tf_op jit(solution)/shard_map/while/body/eval_jaxpr/vmap()/gather | solution.py:29
  77.2 2.9 %convert_element_type.142 = f32[8,8,128,2,128]{4,1,3,2,0:T(8,128)S(1)} convert(bf16[8,8,128,2,128]{4,1,3,2,0:T(8,128)(2,1)} %gather_fusion) | non-fusion elementwise | flops 2097152 | bytes 12582912 | tf_op jit(solution)/shard_map/while/body/eval_jaxpr/vmap()/convert_element_type | solution.py:29
  80.2 3.1 %add_reduce_fusion.2 = (f32[8,128,128]{2,1,0:T(8,128)S(1)}, f32[8,128,128]{2,1,0:T(8,128)S(1)}) fusion(f32[8,8,128,2,128]{4,1,3,2,0:T(8,128)S(1)} %convert_element_type.142, f32[8,128,128]{2,0,1:T(8,128)S(1)} %get-tuple-element.193, f32[8,128,128]{2,0,1:T(8,128)S(1)} %get-tuple-element.194), kind=kLoop, calls=%fused_computation.4.clone.1 | loop fusion | flops 8126464 | bytes 10485760 | tf_op jit(solution)/shard_map/while/body/eval_jaxpr/vmap()/reduce_sum | solution.py:30
  83.3 1.3 constant_dynamic-slice_fusion.2
  84.7 2.2 %copy_dynamic-update-slice_fusion.2 = f32[32,128,2,128]{3,2,0,1:T(2,128)} fusion(f32[32,128,2,128]{3,2,0,1:T(2,128)} %get-tuple-element.207, s32[]{:T(128)S(6)} %select_n.137, f32[8,128,1,128]{3,2,1,0:T(1,128)S(1)} %bitcast.95, f32[8,128,1,128]{3,2,1,0:T(1,128)S(1)} %bitcast.94, f32[8,128,2,128]{3,2,0,1:T(2,128)S(1)} %constant_dynamic-slice_fusion.2), kind=kLoop, calls=%fused_computation.6.clone.1 | loop fusion | flops 524288 | bytes 3145732 | tf_op jit(solution)/shard_map/while/body/eval_jaxpr/dynamic_update_slice | solution.py:42
  86.9 3.1 %gather_fusion = bf16[8,8,128,2,128]{4,1,3,2,0:T(8,128)(2,1)} fusion(bf16[8,256,2,128]{3,0,2,1:T(8,128)(2,1)S(1)} %get-tuple-element.219, s32[8]{0:T(128)S(1)} %fusion.52), kind=kCustom, calls=%fused_computation.clone.1 | custom fusion | bytes 8388736 | tf_op jit(solution)/shard_map/while/body/eval_jaxpr/vmap()/gather | solution.py:29
  90.0 2.9 %convert_element_type.142 = f32[8,8,128,2,128]{4,1,3,2,0:T(8,128)S(1)} convert(bf16[8,8,128,2,128]{4,1,3,2,0:T(8,128)(2,1)} %gather_fusion) | non-fusion elementwise | flops 2097152 | bytes 12582912 | tf_op jit(solution)/shard_map/while/body/eval_jaxpr/vmap()/convert_element_type | solution.py:29
  93.0 3.1 %add_reduce_fusion.2 = (f32[8,128,128]{2,1,0:T(8,128)S(1)}, f32[8,128,128]{2,1,0:T(8,128)S(1)}) fusion(f32[8,8,128,2,128]{4,1,3,2,0:T(8,128)S(1)} %convert_element_type.142, f32[8,128,128]{2,0,1:T(8,128)S(1)} %get-tuple-element.193, f32[8,128,128]{2,0,1:T(8,128)S(1)} %get-tuple-element.194), kind=kLoop, calls=%fused_computation.4.clone.1 | loop fusion | flops 8126464 | bytes 10485760 | tf_op jit(solution)/shard_map/while/body/eval_jaxpr/vmap()/reduce_sum | solution.py:30
  96.1 1.3 constant_dynamic-slice_fusion.2
  97.4 2.2 %copy_dynamic-update-slice_fusion.2 = f32[32,128,2,128]{3,2,0,1:T(2,128)} fusion(f32[32,128,2,128]{3,2,0,1:T(2,128)} %get-tuple-element.207, s32[]{:T(128)S(6)} %select_n.137, f32[8,128,1,128]{3,2,1,0:T(1,128)S(1)} %bitcast.95, f32[8,128,1,128]{3,2,1,0:T(1,128)S(1)} %bitcast.94, f32[8,128,2,128]{3,2,0,1:T(2,128)S(1)} %constant_dynamic-slice_fusion.2), kind=kLoop, calls=%fused_computation.6.clone.1 | loop fusion | flops 524288 | bytes 3145732 | tf_op jit(solution)/shard_map/while/body/eval_jaxpr/dynamic_update_slice | solution.py:42
  99.7 3.1 %gather_fusion = bf16[8,8,128,2,128]{4,1,3,2,0:T(8,128)(2,1)} fusion(bf16[8,256,2,128]{3,0,2,1:T(8,128)(2,1)S(1)} %get-tuple-element.219, s32[8]{0:T(128)S(1)} %fusion.52), kind=kCustom, calls=%fused_computation.clone.1 | custom fusion | bytes 8388736 | tf_op jit(solution)/shard_map/while/body/eval_jaxpr/vmap()/gather | solution.py:29
  102.8 2.9 %convert_element_type.142 = f32[8,8,128,2,128]{4,1,3,2,0:T(8,128)S(1)} convert(bf16[8,8,128,2,128]{4,1,3,2,0:T(8,128)(2,1)} %gather_fusion) | non-fusion elementwise | flops 2097152 | bytes 12582912 | tf_op jit(solution)/shard_map/while/body/eval_jaxpr/vmap()/convert_element_type | solution.py:29
  105.8 3.1 %add_reduce_fusion.2 = (f32[8,128,128]{2,1,0:T(8,128)S(1)}, f32[8,128,128]{2,1,0:T(8,128)S(1)}) fusion(f32[8,8,128,2,128]{4,1,3,2,0:T(8,128)S(1)} %convert_element_type.142, f32[8,128,128]{2,0,1:T(8,128)S(1)} %get-tuple-element.193, f32[8,128,128]{2,0,1:T(8,128)S(1)} %get-tuple-element.194), kind=kLoop, calls=%fused_computation.4.clone.1 | loop fusion | flops 8126464 | bytes 10485760 | tf_op jit(solution)/shard_map/while/body/eval_jaxpr/vmap()/reduce_sum | solution.py:30
  108.9 1.3 constant_dynamic-slice_fusion.2
  110.2 2.2 %copy_dynamic-update-slice_fusion.2 = f32[32,128,2,128]{3,2,0,1:T(2,128)} fusion(f32[32,128,2,128]{3,2,0,1:T(2,128)} %get-tuple-element.207, s32[]{:T(128)S(6)} %select_n.137, f32[8,128,1,128]{3,2,1,0:T(1,128)S(1)} %bitcast.95, f32[8,128,1,128]{3,2,1,0:T(1,128)S(1)} %bitcast.94, f32[8,128,2,128]{3,2,0,1:T(2,128)S(1)} %constant_dynamic-slice_fusion.2), kind=kLoop, calls=%fused_computation.6.clone.1 | loop fusion | flops 524288 | bytes 3145732 | tf_op jit(solution)/shard_map/while/body/eval_jaxpr/dynamic_update_slice | solution.py:42
  112.4 5.5 %convert_element_type.99 = bf16[32,128,2,128]{3,2,0,1:T(2,128)(2,1)} convert(f32[32,128,2,128]{3,2,0,1:T(2,128)} %get-tuple-element.99) | non-fusion elementwise | flops 1048576 | bytes 6291456 | tf_op jit(solution)/shard_map/convert_element_type | solution.py:120
  117.9 3.9 %all-to-all-start.1 = ((bf16[32,128,2,128]{3,2,0,1:T(2,128)(2,1)}), bf16[32,128,2,128]{3,2,0,1:T(2,128)(2,1)S(1)}, u32[]{:S(2)}, u32[]{:S(2)}) async-start(bf16[32,128,2,128]{3,2,0,1:T(2,128)(2,1)} %convert_element_type.99), calls=%async_computation.1 | async-start | bytes 4194304 | tf_op jit(solution)/shard_map/all_to_all | solution.py:124
  121.8 9.8 %cosine_convert_fusion = (bf16[1,1024,512]{2,1,0:T(8,128)(2,1)S(1)}, bf16[1,1024,512]{2,1,0:T(8,128)(2,1)}) fusion(s32[512]{0:T(512)S(1)} %iota_add_fusion, s32[1024]{0:T(1024)S(1)} %copy-done), kind=kLoop, calls=%fused_computation.35 | loop fusion | flops 8912896 | bytes 2103296 | tf_op jit(solution)/shard_map/convert
  131.6 38.9 %all-to-all-done.1 = bf16[32,128,2,128]{3,2,0,1:T(2,128)(2,1)S(1)} async-done(((bf16[32,128,2,128]{3,2,0,1:T(2,128)(2,1)}), bf16[32,128,2,128]{3,2,0,1:T(2,128)(2,1)S(1)}, u32[]{:S(2)}, u32[]{:S(2)}) %all-to-all-start.1) | async-done | bytes 2097184 | tf_op jit(solution)/shard_map/all_to_all | solution.py:124
  170.5 3.8 %copy.79 = bf16[32,8,16,2,128]{4,1,2,3,0:T(8,128)(2,1)} copy(bf16[32,8,16,2,128]{4,3,0,2,1:T(2,128)(2,1)S(1)} %bitcast.96) | data formatting | bytes 4194304 | tf_op jit(solution)/shard_map/all_to_all | solution.py:124
  174.2 2.8 %all_to_all.33 = bf16[32,16,2,1024]{3,1,2,0:T(8,128)(2,1)S(1)} reshape(bf16[32,16,2,8,128]{4,3,1,2,0:T(8,128)(2,1)} %bitcast.97) | data formatting | bytes 4194304 | tf_op jit(solution)/shard_map/all_to_all | solution.py:124
  177.1 3.3 %fusion.14 = bf16[32,16,512]{2,1,0:T(8,128)(2,1)} fusion(bf16[32,16,2,1024]{3,1,2,0:T(8,128)(2,1)S(1)} %all_to_all.33, bf16[1,1024,512]{2,1,0:T(8,128)(2,1)} %get-tuple-element.151, bf16[1,1024,512]{2,1,0:T(8,128)(2,1)S(1)} %get-tuple-element.150), kind=kOutput, calls=%fused_computation.39 | convolution fusion | flops 1075314688 | bytes 4718592 | tf_op jit(solution)/shard_map/ocpk,pkl->ocl/dot_general | solution.py:122
  (26 shorter events, 2.3 us)
Async XLA Ops:
  28.7 11.2 %copy-start.1 = (s32[128]{0:T(128)S(1)}, s32[128]{0:T(128)}, u32[]{:S(2)}) copy-start(s32[128]{0:T(128)} %param.7) | copy-start | bytes 1540
  32.7 14.6 %all-to-all-start = ((bf16[8,2,4096]{2,1,0:T(2,128)(2,1)}), bf16[8,2,4096]{2,1,0:T(2,128)(2,1)S(1)}, u32[]{:S(2)}, u32[]{:S(2)}) async-start(bf16[8,2,4096]{2,1,0:T(2,128)(2,1)} %reshape.414), calls=%async_computation | async-start | bytes 262144 | tf_op jit(solution)/shard_map/all_to_all | solution.py:107
  112.4 9.4 %copy-start = (s32[1024]{0:T(1024)S(1)}, s32[1024]{0:T(1024)}, u32[]{:S(2)}) copy-start(s32[1024]{0:T(1024)} %param.6) | copy-start | bytes 12292
  117.9 52.6 %all-to-all-start.1 = ((bf16[32,128,2,128]{3,2,0,1:T(2,128)(2,1)}), bf16[32,128,2,128]{3,2,0,1:T(2,128)(2,1)S(1)}, u32[]{:S(2)}, u32[]{:S(2)}) async-start(bf16[32,128,2,128]{3,2,0,1:T(2,128)(2,1)} %convert_element_type.99), calls=%async_computation.1 | async-start | bytes 4194304 | tf_op jit(solution)/shard_map/all_to_all | solution.py:124
where the time goes:
time: 181 us; the launch traced here: 180 us
  other arithmetic  63.3 us (35%)
  waiting for transfers between devices  46.1 us (25%)
  local copies, waits for them, and re-layouts  43.5 us (24%)
  starting transfers between devices  11.1 us (6%)
  matrix products  8.83 us (5%)
  blocking collectives  7.18 us (4%)
    all_to_all x1, waiting for transfers between devices, local(): lax.all_to_all(cross_sum, 'gx', split_axis=1, concat_axis=3, tiled=True)  38.9 us
    reduce_sum x4, other arithmetic, one_offset(): jnp.sum(own_part[:, :, 0] * theirs[:, :, 0] + own_part[:, :, 1] * theirs[...  12.3 us
    gather x4, local copies, waits for them, and re-layouts, one_offset(): lax.dynamic_slice_in_dim(window_block, shift_by, own_count, 1)  12.2 us
    convert_element_type x4, other arithmetic, one_offset(): lax.dynamic_slice_in_dim(window_block, shift_by, own_count, 1)  11.7 us
    another operation x2, other arithmetic  11.3 us
    dynamic_update_slice x4, other arithmetic, one_group(): lax.dynamic_update_slice_in_dim(carried, current + update, group_index *...  8.78 us
    all_to_all x1, starting transfers between devices, local(): lax.all_to_all(white, 'gx', split_axis=3, concat_axis=1, tiled=True)  7.27 us
    all_to_all x1, waiting for transfers between devices, local(): lax.all_to_all(white, 'gx', split_axis=3, concat_axis=1, tiled=True)  7.26 us
  transfers between devices with their start and end apart: 2, of which 2 were waited for; matrix products, arithmetic and copies ran while one was open for 5% of the time, Pallas kernels for 0%

commit v1 on v0

--- a/solution.py
+++ b/solution.py
@@ -107,7 +107,12 @@
     freq_white = lax.all_to_all(white, "gx", split_axis=3, concat_axis=1, tiled=True)
     all_channels = freq_white.shape[1]
     empty_sum = jnp.zeros((off_dev, all_channels, 2, freq_white.shape[3]), jnp.float32)
-    window_block = lax.all_gather(freq_white, "gy", axis=0, tiled=True)
+    ring = [freq_white]
+    for hop in range(3):
+        ring.append(lax.ppermute(ring[-1], "gy", [(dev, (dev + 1) % 4) for dev in range(4)]))
+    window_block = jnp.roll(
+        jnp.concatenate(ring[::-1], axis=0), (lax.axis_index("gy") + 1) * ring[0].shape[0], axis=0
+    )
     widened = jnp.concatenate(
         [
             window_block,

time: 181 us -> 185 us (1.022)
  blocking collectives: 7.18 us -> 14.4 us
  starting transfers between devices: 11.1 us -> 3.92 us
  waiting for transfers between devices: 46.1 us -> 50.8 us
    all_to_all x0 -> x1, blocking collectives: none -> 14.4 us  [local(): lax.all_to_all(white, 'gx', split_axis=3, concat_axis=1, tiled=True)]
    ppermute x0 -> x3, waiting for transfers between devices: none -> 13.1 us  [local(): lax.ppermute(ring[-1], 'gy', [(dev, (dev + 1) % 4) for dev in range(4)])]
    all_to_all x1 -> x0, starting transfers between devices: 7.27 us -> none  [local(): lax.all_to_all(white, 'gx', split_axis=3, concat_axis=1, tiled=True)]
    all_to_all x1 -> x0, waiting for transfers between devices: 7.26 us -> none  [local(): lax.all_to_all(white, 'gx', split_axis=3, concat_axis=1, tiled=True)]
    all_gather x1 -> x0, blocking collectives: 7.18 us -> none  [local(): window_block = lax.all_gather(freq_white, 'gy', axis=0, tiled=True)]
  transfers between devices with their start and end apart: 2 -> 4, of which waited for: 2 -> 4; matrix products, arithmetic and copies ran while one was open for 5% -> 5% of each run, Pallas kernels for 0% -> 0%
where the time goes in v1:
time: 185 us
  other arithmetic  63.3 us (34%)
  waiting for transfers between devices  50.8 us (27%)
  local copies, waits for them, and re-layouts  43 us (23%)
  blocking collectives  14.4 us (8%)
  matrix products  8.83 us (5%)
  starting transfers between devices  3.92 us (2%)
    all_to_all x1, waiting for transfers between devices, local(): lax.all_to_all(cross_sum, 'gx', split_axis=1, concat_axis=3, tiled=True)  37.7 us
    all_to_all x1, blocking collectives, local(): lax.all_to_all(white, 'gx', split_axis=3, concat_axis=1, tiled=True)  14.4 us
    ppermute x3, waiting for transfers between devices, local(): lax.ppermute(ring[-1], 'gy', [(dev, (dev + 1) % 4) for dev in range(4)])  13.1 us
    reduce_sum x4, other arithmetic, one_offset(): jnp.sum(own_part[:, :, 0] * theirs[:, :, 0] + own_part[:, :, 1] * theirs[...  12.3 us
    gather x4, local copies, waits for them, and re-layouts, one_offset(): lax.dynamic_slice_in_dim(window_block, shift_by, own_count, 1)  12.2 us
    convert_element_type x4, other arithmetic, one_offset(): lax.dynamic_slice_in_dim(window_block, shift_by, own_count, 1)  11.7 us
    another operation x2, other arithmetic  11.3 us
    dynamic_update_slice x4, other arithmetic, one_group(): lax.dynamic_update_slice_in_dim(carried, current + update, group_index *...  8.8 us
  transfers between devices with their start and end apart: 4, of which 4 were waited for; matrix products, arithmetic and copies ran while one was open for 5% of the time, Pallas kernels for 0%

profile of v1, /device:TPU:0, one launch (start us, length us, event | category | flops | bytes accessed | tf_op | source)
XLA Modules:
  0.0 184.6 jit_solution(1332663557886934912)
XLA Ops:
  0.1 0.7 add_select_fusion.4
  0.8 1.7 fusion.32
  2.5 1.3 copy.39
  4.1 1.0 convert_bitcast_fusion
  5.4 1.2 copy.40
  6.5 1.5 subtract_convert_fusion
  8.0 4.5 %fusion.2 = f32[1024,2048]{1,0:T(8,128)S(1)} fusion(bf16[1024,1024]{1,0:T(8,128)(2,1)S(1)} %bitcast.101, bf16[1024,1024]{1,0:T(8,128)(2,1)S(1)} %bitcast.103, bf16[1024,1024]{1,0:T(8,128)(2,1)S(1)} %bitcast.102), kind=kOutput, calls=%fused_computation.14 | convolution fusion | flops 4303355904 | bytes 14680064 | tf_op jit(solution)/shard_map/dot_general | solution.py:84
  12.6 2.7 %slice_add_fusion = f32[512,2048]{1,0:T(8,128)} fusion(f32[1024,2048]{1,0:T(8,128)S(1)} %fusion.2), kind=kLoop, calls=%fused_computation.13 | loop fusion | flops 1048576 | bytes 12582912 | tf_op jit(solution)/shard_map/add | solution.py:86
  15.3 6.6 %add.170 = f32[2,8,32,2,1024]{4,3,2,1,0:T(2,128)} reshape(f32[512,2048]{1,0:T(8,128)} %slice_add_fusion) | data formatting | bytes 8388608 | tf_op jit(solution)/shard_map/add | solution.py:86
  21.9 6.9 %slice_add_fusion.1 = (f32[1,8,32,1,1024]{4,3,2,1,0:T(1,128)S(1)}, f32[1,8,32,1,1024]{4,3,2,1,0:T(1,128)S(1)}, f32[1,8,32,1,1024]{4,3,2,1,0:T(1,128)S(1)}) fusion(f32[2,8,32,2,1024]{4,3,2,1,0:T(2,128)} %add.170), kind=kLoop, calls=%fused_computation.41 | loop fusion | flops 262144 | bytes 7340032 | tf_op jit(solution)/shard_map/add | solution.py:92
  28.7 0.8 fusion.18
  30.1 0.8 copy.43
  31.0 1.1 reshape.414
  32.0 14.4 %all_to_all.36 = bf16[8,2,4096]{2,1,0:T(2,128)(2,1)S(1)} all-to-all(bf16[8,2,4096]{2,1,0:T(2,128)(2,1)S(1)} %reshape.414), channel_id=1, replica_groups=mesh['gx'=8,'gy'=4] {'gx'}, dimensions={0} | all-to-all | bytes 262144 | tf_op jit(solution)/shard_map/all_to_all | solution.py:107
  46.4 0.7 reshape.415
  47.1 1.3 copy.53
  48.5 4.4 %collective-permute-done = bf16[2,128,2,128]{3,1,2,0:T(8,128)(2,1)S(1)} collective-permute-done((bf16[2,128,2,128]{3,1,2,0:T(8,128)(2,1)S(1)}, bf16[2,128,2,128]{3,1,2,0:T(8,128)(2,1)S(1)}, u32[]{:S(2)}, u32[]{:S(2)}) %collective-permute-start) | collective-permute-done | bytes 131104 | tf_op jit(solution)/shard_map/ppermute | solution.py:112
  52.9 4.4 %collective-permute-done.1 = bf16[2,128,2,128]{3,1,2,0:T(8,128)(2,1)S(1)} collective-permute-done((bf16[2,128,2,128]{3,1,2,0:T(8,128)(2,1)S(1)}, bf16[2,128,2,128]{3,1,2,0:T(8,128)(2,1)S(1)}, u32[]{:S(2)}, u32[]{:S(2)}) %collective-permute-start.1) | collective-permute-done | bytes 131104 | tf_op jit(solution)/shard_map/ppermute | solution.py:112
  57.4 4.3 %collective-permute-done.2 = bf16[2,128,2,128]{3,1,2,0:T(8,128)(2,1)S(1)} collective-permute-done((bf16[2,128,2,128]{3,1,2,0:T(8,128)(2,1)S(1)}, bf16[2,128,2,128]{3,1,2,0:T(8,128)(2,1)S(1)}, u32[]{:S(2)}, u32[]{:S(2)}) %collective-permute-start.2) | collective-permute-done | bytes 131104 | tf_op jit(solution)/shard_map/ppermute | solution.py:112
  62.8 4.0 %broadcast_in_dim.8.clone = f32[32,128,2,128]{3,2,0,1:T(2,128)} broadcast(f32[]{:T(128)} %constant.125.clone.1), dimensions={} | broadcast | bytes 4194308 | tf_op jit(solution)/shard_map/broadcast_in_dim | solution.py:109
  66.8 51.1 %while.13 = (s32[]{:T(128)}, f32[32,128,2,128]{3,2,0,1:T(2,128)}, f32[8,128,2,128]{3,0,1,2:T(8,128)S(1)}, s32[32]{0:T(128)S(1)}, bf16[8,256,2,128]{3,0,2,1:T(8,1...) while((s32[]{:T(128)}, f32[32,128,2,128]{3,2,0,1:T(2,128)}, ...), condition=%wide.region_6.7_spmd, body=%wide.region_3.6_spmd.sunk | while | flops 10747950 | bytes 38797656 | solution.py:46
  66.9 3.1 %gather_fusion = bf16[8,8,128,2,128]{4,1,3,2,0:T(8,128)(2,1)} fusion(bf16[8,256,2,128]{3,0,2,1:T(8,128)(2,1)S(1)} %get-tuple-element.219, s32[8]{0:T(128)S(1)} %fusion.52), kind=kCustom, calls=%fused_computation.clone.1 | custom fusion | bytes 8388736 | tf_op jit(solution)/shard_map/while/body/eval_jaxpr/vmap()/gather | solution.py:29
  69.9 2.9 %convert_element_type.142 = f32[8,8,128,2,128]{4,1,3,2,0:T(8,128)S(1)} convert(bf16[8,8,128,2,128]{4,1,3,2,0:T(8,128)(2,1)} %gather_fusion) | non-fusion elementwise | flops 2097152 | bytes 12582912 | tf_op jit(solution)/shard_map/while/body/eval_jaxpr/vmap()/convert_element_type | solution.py:29
  73.0 3.1 %add_reduce_fusion.2 = (f32[8,128,128]{2,1,0:T(8,128)S(1)}, f32[8,128,128]{2,1,0:T(8,128)S(1)}) fusion(f32[8,8,128,2,128]{4,1,3,2,0:T(8,128)S(1)} %convert_element_type.142, f32[8,128,128]{2,0,1:T(8,128)S(1)} %get-tuple-element.193, f32[8,128,128]{2,0,1:T(8,128)S(1)} %get-tuple-element.194), kind=kLoop, calls=%fused_computation.4.clone.1 | loop fusion | flops 8126464 | bytes 10485760 | tf_op jit(solution)/shard_map/while/body/eval_jaxpr/vmap()/reduce_sum | solution.py:30
  76.1 1.3 constant_dynamic-slice_fusion.3
  77.4 2.2 %copy_dynamic-update-slice_fusion.2 = f32[32,128,2,128]{3,2,0,1:T(2,128)} fusion(f32[32,128,2,128]{3,2,0,1:T(2,128)} %get-tuple-element.207, s32[]{:T(128)S(6)} %select_n.151, f32[8,128,1,128]{3,2,1,0:T(1,128)S(1)} %bitcast.95, f32[8,128,1,128]{3,2,1,0:T(1,128)S(1)} %bitcast.94, f32[8,128,2,128]{3,2,0,1:T(2,128)S(1)} %constant_dynamic-slice_fusion.3), kind=kLoop, calls=%fused_computation.6.clone.1 | loop fusion | flops 524288 | bytes 3145732 | tf_op jit(solution)/shard_map/while/body/eval_jaxpr/dynamic_update_slice | solution.py:42
  79.7 3.1 %gather_fusion = bf16[8,8,128,2,128]{4,1,3,2,0:T(8,128)(2,1)} fusion(bf16[8,256,2,128]{3,0,2,1:T(8,128)(2,1)S(1)} %get-tuple-element.219, s32[8]{0:T(128)S(1)} %fusion.52), kind=kCustom, calls=%fused_computation.clone.1 | custom fusion | bytes 8388736 | tf_op jit(solution)/shard_map/while/body/eval_jaxpr/vmap()/gather | solution.py:29
  82.7 2.9 %convert_element_type.142 = f32[8,8,128,2,128]{4,1,3,2,0:T(8,128)S(1)} convert(bf16[8,8,128,2,128]{4,1,3,2,0:T(8,128)(2,1)} %gather_fusion) | non-fusion elementwise | flops 2097152 | bytes 12582912 | tf_op jit(solution)/shard_map/while/body/eval_jaxpr/vmap()/convert_element_type | solution.py:29
  85.7 3.1 %add_reduce_fusion.2 = (f32[8,128,128]{2,1,0:T(8,128)S(1)}, f32[8,128,128]{2,1,0:T(8,128)S(1)}) fusion(f32[8,8,128,2,128]{4,1,3,2,0:T(8,128)S(1)} %convert_element_type.142, f32[8,128,128]{2,0,1:T(8,128)S(1)} %get-tuple-element.193, f32[8,128,128]{2,0,1:T(8,128)S(1)} %get-tuple-element.194), kind=kLoop, calls=%fused_computation.4.clone.1 | loop fusion | flops 8126464 | bytes 10485760 | tf_op jit(solution)/shard_map/while/body/eval_jaxpr/vmap()/reduce_sum | solution.py:30
  88.8 1.3 constant_dynamic-slice_fusion.3
  90.2 2.2 %copy_dynamic-update-slice_fusion.2 = f32[32,128,2,128]{3,2,0,1:T(2,128)} fusion(f32[32,128,2,128]{3,2,0,1:T(2,128)} %get-tuple-element.207, s32[]{:T(128)S(6)} %select_n.151, f32[8,128,1,128]{3,2,1,0:T(1,128)S(1)} %bitcast.95, f32[8,128,1,128]{3,2,1,0:T(1,128)S(1)} %bitcast.94, f32[8,128,2,128]{3,2,0,1:T(2,128)S(1)} %constant_dynamic-slice_fusion.3), kind=kLoop, calls=%fused_computation.6.clone.1 | loop fusion | flops 524288 | bytes 3145732 | tf_op jit(solution)/shard_map/while/body/eval_jaxpr/dynamic_update_slice | solution.py:42
  92.4 3.1 %gather_fusion = bf16[8,8,128,2,128]{4,1,3,2,0:T(8,128)(2,1)} fusion(bf16[8,256,2,128]{3,0,2,1:T(8,128)(2,1)S(1)} %get-tuple-element.219, s32[8]{0:T(128)S(1)} %fusion.52), kind=kCustom, calls=%fused_computation.clone.1 | custom fusion | bytes 8388736 | tf_op jit(solution)/shard_map/while/body/eval_jaxpr/vmap()/gather | solution.py:29
  95.5 2.9 %convert_element_type.142 = f32[8,8,128,2,128]{4,1,3,2,0:T(8,128)S(1)} convert(bf16[8,8,128,2,128]{4,1,3,2,0:T(8,128)(2,1)} %gather_fusion) | non-fusion elementwise | flops 2097152 | bytes 12582912 | tf_op jit(solution)/shard_map/while/body/eval_jaxpr/vmap()/convert_element_type | solution.py:29
  98.5 3.1 %add_reduce_fusion.2 = (f32[8,128,128]{2,1,0:T(8,128)S(1)}, f32[8,128,128]{2,1,0:T(8,128)S(1)}) fusion(f32[8,8,128,2,128]{4,1,3,2,0:T(8,128)S(1)} %convert_element_type.142, f32[8,128,128]{2,0,1:T(8,128)S(1)} %get-tuple-element.193, f32[8,128,128]{2,0,1:T(8,128)S(1)} %get-tuple-element.194), kind=kLoop, calls=%fused_computation.4.clone.1 | loop fusion | flops 8126464 | bytes 10485760 | tf_op jit(solution)/shard_map/while/body/eval_jaxpr/vmap()/reduce_sum | solution.py:30
  101.6 1.3 constant_dynamic-slice_fusion.3
  102.9 2.2 %copy_dynamic-update-slice_fusion.2 = f32[32,128,2,128]{3,2,0,1:T(2,128)} fusion(f32[32,128,2,128]{3,2,0,1:T(2,128)} %get-tuple-element.207, s32[]{:T(128)S(6)} %select_n.151, f32[8,128,1,128]{3,2,1,0:T(1,128)S(1)} %bitcast.95, f32[8,128,1,128]{3,2,1,0:T(1,128)S(1)} %bitcast.94, f32[8,128,2,128]{3,2,0,1:T(2,128)S(1)} %constant_dynamic-slice_fusion.3), kind=kLoop, calls=%fused_computation.6.clone.1 | loop fusion | flops 524288 | bytes 3145732 | tf_op jit(solution)/shard_map/while/body/eval_jaxpr/dynamic_update_slice | solution.py:42
  105.2 3.1 %gather_fusion = bf16[8,8,128,2,128]{4,1,3,2,0:T(8,128)(2,1)} fusion(bf16[8,256,2,128]{3,0,2,1:T(8,128)(2,1)S(1)} %get-tuple-element.219, s32[8]{0:T(128)S(1)} %fusion.52), kind=kCustom, calls=%fused_computation.clone.1 | custom fusion | bytes 8388736 | tf_op jit(solution)/shard_map/while/body/eval_jaxpr/vmap()/gather | solution.py:29
  108.2 2.9 %convert_element_type.142 = f32[8,8,128,2,128]{4,1,3,2,0:T(8,128)S(1)} convert(bf16[8,8,128,2,128]{4,1,3,2,0:T(8,128)(2,1)} %gather_fusion) | non-fusion elementwise | flops 2097152 | bytes 12582912 | tf_op jit(solution)/shard_map/while/body/eval_jaxpr/vmap()/convert_element_type | solution.py:29
  111.3 3.1 %add_reduce_fusion.2 = (f32[8,128,128]{2,1,0:T(8,128)S(1)}, f32[8,128,128]{2,1,0:T(8,128)S(1)}) fusion(f32[8,8,128,2,128]{4,1,3,2,0:T(8,128)S(1)} %convert_element_type.142, f32[8,128,128]{2,0,1:T(8,128)S(1)} %get-tuple-element.193, f32[8,128,128]{2,0,1:T(8,128)S(1)} %get-tuple-element.194), kind=kLoop, calls=%fused_computation.4.clone.1 | loop fusion | flops 8126464 | bytes 10485760 | tf_op jit(solution)/shard_map/while/body/eval_jaxpr/vmap()/reduce_sum | solution.py:30
  114.4 1.3 constant_dynamic-slice_fusion.3
  115.7 2.2 %copy_dynamic-update-slice_fusion.2 = f32[32,128,2,128]{3,2,0,1:T(2,128)} fusion(f32[32,128,2,128]{3,2,0,1:T(2,128)} %get-tuple-element.207, s32[]{:T(128)S(6)} %select_n.151, f32[8,128,1,128]{3,2,1,0:T(1,128)S(1)} %bitcast.95, f32[8,128,1,128]{3,2,1,0:T(1,128)S(1)} %bitcast.94, f32[8,128,2,128]{3,2,0,1:T(2,128)S(1)} %constant_dynamic-slice_fusion.3), kind=kLoop, calls=%fused_computation.6.clone.1 | loop fusion | flops 524288 | bytes 3145732 | tf_op jit(solution)/shard_map/while/body/eval_jaxpr/dynamic_update_slice | solution.py:42
  117.9 5.5 %convert_element_type.99 = bf16[32,128,2,128]{3,2,0,1:T(2,128)(2,1)} convert(f32[32,128,2,128]{3,2,0,1:T(2,128)} %get-tuple-element.99) | non-fusion elementwise | flops 1048576 | bytes 6291456 | tf_op jit(solution)/shard_map/convert_element_type | solution.py:125
  123.4 3.9 %all-to-all-start.1 = ((bf16[32,128,2,128]{3,2,0,1:T(2,128)(2,1)}), bf16[32,128,2,128]{3,2,0,1:T(2,128)(2,1)S(1)}, u32[]{:S(2)}, u32[]{:S(2)}) async-start(bf16[32,128,2,128]{3,2,0,1:T(2,128)(2,1)} %convert_element_type.99), calls=%async_computation.1 | async-start | bytes 4194304 | tf_op jit(solution)/shard_map/all_to_all | solution.py:129
  127.3 9.8 %cosine_convert_fusion = (bf16[1,1024,512]{2,1,0:T(8,128)(2,1)S(1)}, bf16[1,1024,512]{2,1,0:T(8,128)(2,1)}) fusion(s32[512]{0:T(512)S(1)} %iota_add_fusion, s32[1024]{0:T(1024)S(1)} %copy-done), kind=kLoop, calls=%fused_computation.35 | loop fusion | flops 8912896 | bytes 2103296 | tf_op jit(solution)/shard_map/convert
  137.1 37.7 %all-to-all-done.1 = bf16[32,128,2,128]{3,2,0,1:T(2,128)(2,1)S(1)} async-done(((bf16[32,128,2,128]{3,2,0,1:T(2,128)(2,1)}), bf16[32,128,2,128]{3,2,0,1:T(2,128)(2,1)S(1)}, u32[]{:S(2)}, u32[]{:S(2)}) %all-to-all-start.1) | async-done | bytes 2097184 | tf_op jit(solution)/shard_map/all_to_all | solution.py:129
  174.8 3.8 %copy.79 = bf16[32,8,16,2,128]{4,1,2,3,0:T(8,128)(2,1)} copy(bf16[32,8,16,2,128]{4,3,0,2,1:T(2,128)(2,1)S(1)} %bitcast.96) | data formatting | bytes 4194304 | tf_op jit(solution)/shard_map/all_to_all | solution.py:129
  178.5 2.8 %all_to_all.33 = bf16[32,16,2,1024]{3,1,2,0:T(8,128)(2,1)S(1)} reshape(bf16[32,16,2,8,128]{4,3,1,2,0:T(8,128)(2,1)} %bitcast.97) | data formatting | bytes 4194304 | tf_op jit(solution)/shard_map/all_to_all | solution.py:129
  181.3 3.3 %fusion.14 = bf16[32,16,512]{2,1,0:T(8,128)(2,1)} fusion(bf16[32,16,2,1024]{3,1,2,0:T(8,128)(2,1)S(1)} %all_to_all.33, bf16[1,1024,512]{2,1,0:T(8,128)(2,1)} %get-tuple-element.151, bf16[1,1024,512]{2,1,0:T(8,128)(2,1)S(1)} %get-tuple-element.150), kind=kOutput, calls=%fused_computation.39 | convolution fusion | flops 1075314688 | bytes 4718592 | tf_op jit(solution)/shard_map/ocpk,pkl->ocl/dot_general | solution.py:127
  (39 shorter events, 2.9 us)
Async XLA Ops:
  28.7 28.6 %copy-start.1 = (s32[128]{0:T(128)S(1)}, s32[128]{0:T(128)}, u32[]{:S(2)}) copy-start(s32[128]{0:T(128)} %param.7) | copy-start | bytes 1540
  48.4 4.4 %collective-permute-start = (bf16[2,128,2,128]{3,1,2,0:T(8,128)(2,1)S(1)}, bf16[2,128,2,128]{3,1,2,0:T(8,128)(2,1)S(1)}, u32[]{:S(2)}, u32[]{:S(2)}) collective-permute-start(bf16[2,128,2,128]{3,1,2,0:T(8,128)(2,1)S(1)} %bitcast.105), channel_id=1, source_target_pairs={{0,1},{1,2},{2,3},{3,0},{4,5},{5,6},{6,7},{7,4},{8,9},{9,10},{10,1... | collective-permute-start | bytes 393224 | tf_op jit(solution)/shard_map/ppermute | solution.py:112
  52.9 4.4 %collective-permute-start.1 = (bf16[2,128,2,128]{3,1,2,0:T(8,128)(2,1)S(1)}, bf16[2,128,2,128]{3,1,2,0:T(8,128)(2,1)S(1)}, u32[]{:S(2)}, u32[]{:S(2)}) collective-permute-start(bf16[2,128,2,128]{3,1,2,0:T(8,128)(2,1)S(1)} %collective-permute-done), channel_id=1, source_target_pairs={{0,1},{1,2},{2,3},{3,0},{4,5},{5,6},{6,7},{7,4},{8,9},{9,10},{10,1... | collective-permute-start | bytes 393224 | tf_op jit(solution)/shard_map/ppermute | solution.py:112
  57.3 4.4 %collective-permute-start.2 = (bf16[2,128,2,128]{3,1,2,0:T(8,128)(2,1)S(1)}, bf16[2,128,2,128]{3,1,2,0:T(8,128)(2,1)S(1)}, u32[]{:S(2)}, u32[]{:S(2)}) collective-permute-start(bf16[2,128,2,128]{3,1,2,0:T(8,128)(2,1)S(1)} %collective-permute-done.1), channel_id=1, source_target_pairs={{0,1},{1,2},{2,3},{3,0},{4,5},{5,6},{6,7},{7,4},{8,9},{9,10},{10,1... | collective-permute-start | bytes 393224 | tf_op jit(solution)/shard_map/ppermute | solution.py:112
  117.9 9.4 %copy-start = (s32[1024]{0:T(1024)S(1)}, s32[1024]{0:T(1024)}, u32[]{:S(2)}) copy-start(s32[1024]{0:T(1024)} %param.6) | copy-start | bytes 12292
  123.4 51.4 %all-to-all-start.1 = ((bf16[32,128,2,128]{3,2,0,1:T(2,128)(2,1)}), bf16[32,128,2,128]{3,2,0,1:T(2,128)(2,1)S(1)}, u32[]{:S(2)}, u32[]{:S(2)}) async-start(bf16[32,128,2,128]{3,2,0,1:T(2,128)(2,1)} %convert_element_type.99), calls=%async_computation.1 | async-start | bytes 4194304 | tf_op jit(solution)/shard_map/all_to_all | solution.py:129
